TPU v7x, 32 devices: a whole 2x2x4 slice. The times are simulated.
32 devices in a mesh: dp: 4 (over y, x), expert: 8 (over z, core).
Axes of the slice: x: 2, y: 2, z: 4, core: 2. Of those that a mesh axis runs over, the one named last changes fastest.
Arguments:
- tokens: bfloat16 [4096, 4096], P(('dp', 'expert')), may hold values from -6 to 6
- expert_ids: int32 [4096, 2], P(('dp', 'expert')), may hold values from 0 to 7, all different within a row; in each aligned block of 128 rows (0 to 127, 128 to 255, ...) at most 64 rows name the same one
- combine: float32 [4096, 2], P(('dp', 'expert')), may hold values from 0.2 to 1
- weight_gate: bfloat16 [8, 768, 4096], P('expert'), may hold values from -0.09375 to 0.09375
- weight_up: bfloat16 [8, 768, 4096], P('expert'), may hold values from -0.09375 to 0.09375
- weight_down: bfloat16 [8, 768, 4096], P('expert'), may hold values from -0.21875 to 0.21875
- grad_out: bfloat16 [4096, 4096], P(('dp', 'expert')), may hold values from -6 to 6
Outputs:
- mixed: bfloat16 [4096, 4096], P(('dp', 'expert'))
- grad_tokens: bfloat16 [4096, 4096], P(('dp', 'expert'))
- grad_combine: float32 [4096, 2], P(('dp', 'expert'))
- grad_gate: bfloat16 [8, 768, 4096], P('expert', 'dp')
- grad_up: bfloat16 [8, 768, 4096], P('expert', 'dp')
- grad_down: bfloat16 [8, 768, 4096], P('expert', 'dp')
Inputs may be any that keep to these rules, and one draw needn't show every extreme that they name: `expert_ids`: each row names 2 different experts. In the rows of one device no expert is named more than 64 times, a bound that some block reaches.
All inputs are finite; a program needn't handle non-finite values.
Results may differ from a plain program's by a relative error of at most 0.012.
Values may be sent and summed in bfloat16 or wider, within the bound.
No kernel may reach another device: no remote copies, remote signals or barrier semaphores. Data moves between devices by JAX's collectives and lax.ppermute only.
A program may use at most 192 MiB of HBM per device.

v0:
```python
import jax
import jax.numpy as jnp
from jax import lax
from jax.sharding import PartitionSpec as P


def slot_targets(expert_ids, experts, capacity):
    tok_count, top_count = expert_ids.shape
    pair_total = tok_count * top_count
    flat_ids = expert_ids.reshape(pair_total)
    onehot = (flat_ids[:, None] == jnp.arange(experts, dtype=jnp.int32)[None, :]).astype(jnp.int32)
    earlier = jnp.cumsum(onehot, axis=0) - onehot
    position = jnp.sum(earlier * onehot, axis=1)
    return (flat_ids * capacity + position).reshape(tok_count, top_count)


def per_device(tokens, expert_ids, combine, weight_gate, weight_up, weight_down, grad_out):
    tok_count, top_count = expert_ids.shape
    model_width = tokens.shape[1]
    experts = lax.axis_size("expert")
    copies = lax.axis_size("dp")
    capacity = 2 * tok_count * top_count // experts
    slots = experts * capacity
    target = slot_targets(expert_ids, experts, capacity)
    slot_iota = jnp.arange(slots, dtype=jnp.int32)
    hit = target.T[:, :, None] == slot_iota[None, None, :]
    send_onehot = jnp.any(hit, axis=0).T.astype(jnp.bfloat16)
    weight_pair = jnp.sum(
        jnp.where(hit, combine.T[:, :, None], jnp.zeros((), jnp.float32)), axis=(0, 1)
    )
    with jax.named_scope("dispatch_rows"):
        send_rows = jnp.dot(send_onehot, tokens, preferred_element_type=jnp.float32).astype(
            jnp.bfloat16
        )
        send_go = jnp.dot(send_onehot, grad_out, preferred_element_type=jnp.float32)
        send_grads = (weight_pair[:, None] * send_go).astype(jnp.bfloat16)
    send_rows = send_rows.reshape(experts, capacity, model_width)
    send_grads = send_grads.reshape(experts, capacity, model_width)
    recv_rows = lax.all_to_all(send_rows, "expert", split_axis=0, concat_axis=0, tiled=True)
    recv_rows, send_grads = lax.optimization_barrier((recv_rows, send_grads))
    recv_grads = lax.all_to_all(send_grads, "expert", split_axis=0, concat_axis=0, tiled=True)
    in_rows = recv_rows.reshape(slots, model_width)
    out_grads = recv_grads.reshape(slots, model_width)
    w_gate = weight_gate[0]
    w_up = weight_up[0]
    w_down = weight_down[0]

    def forward(rows):
        gate_pre = jnp.dot(rows, w_gate.T, preferred_element_type=jnp.float32)
        up_pre = jnp.dot(rows, w_up.T, preferred_element_type=jnp.float32)
        sigmoid_gate = jax.nn.sigmoid(gate_pre)
        activated = (gate_pre * sigmoid_gate * up_pre).astype(jnp.bfloat16)
        expert_out = jnp.dot(activated, w_down, preferred_element_type=jnp.float32).astype(
            jnp.bfloat16
        )
        return (gate_pre, up_pre, sigmoid_gate, activated, expert_out)

    always = expert_ids[0, 0] >= 0
    gate_pre, up_pre, sigmoid_gate, activated, expert_out = lax.cond(
        always, forward, forward, in_rows
    )
    back_out = lax.all_to_all(
        expert_out.reshape(experts, capacity, model_width),
        "expert",
        split_axis=0,
        concat_axis=0,
        tiled=True,
    )
    scale = (tok_count * top_count * copies) ** (-0.5)
    grad_act = jnp.dot(out_grads, w_down.T, preferred_element_type=jnp.float32)
    grad_gate_pre = (
        grad_act * up_pre * sigmoid_gate * (1.0 + gate_pre * (1.0 - sigmoid_gate))
    ).astype(jnp.bfloat16)
    grad_up_pre = (grad_act * gate_pre * sigmoid_gate).astype(jnp.bfloat16)
    row_grads = (
        jnp.dot(grad_gate_pre, w_gate, preferred_element_type=jnp.float32)
        + jnp.dot(grad_up_pre, w_up, preferred_element_type=jnp.float32)
    ).astype(jnp.bfloat16)
    back_grads = lax.all_to_all(
        row_grads.reshape(experts, capacity, model_width),
        "expert",
        split_axis=0,
        concat_axis=0,
        tiled=True,
    )
    ff_share = w_gate.shape[0] // copies
    with jax.named_scope("weight_grads"):
        down_term = (
            scale
            * jnp.einsum("rf,rd->fd", activated, out_grads, preferred_element_type=jnp.float32)
        ).astype(jnp.bfloat16)
        rows_all = lax.all_gather(in_rows, "dp", axis=0, tiled=True)
        grads_pre = jnp.concatenate([grad_gate_pre, grad_up_pre], axis=1)
        grads_all = lax.all_gather(grads_pre, "dp", axis=0, tiled=True)
        me_dp = lax.axis_index("dp")
        ff = w_gate.shape[0]
        gate_cols = lax.dynamic_slice_in_dim(grads_all, me_dp * ff_share, ff_share, 1)
        up_cols = lax.dynamic_slice_in_dim(grads_all, ff + me_dp * ff_share, ff_share, 1)
        gate_share = (
            scale * jnp.einsum("rf,rd->fd", gate_cols, rows_all, preferred_element_type=jnp.float32)
        ).astype(jnp.bfloat16)
        up_share = (
            scale * jnp.einsum("rf,rd->fd", up_cols, rows_all, preferred_element_type=jnp.float32)
        ).astype(jnp.bfloat16)
    down_share = lax.psum_scatter(down_term, "dp", scatter_dimension=0, tiled=True)
    pick_onehot = hit.reshape(top_count * tok_count, slots).astype(jnp.bfloat16)
    with jax.named_scope("combine_rows"):
        picked_out = jnp.dot(
            pick_onehot, back_out.reshape(slots, model_width), preferred_element_type=jnp.float32
        ).reshape(top_count, tok_count, model_width)
        grad_f32 = grad_out.astype(jnp.float32)
        mixed = combine[:, 0:1] * picked_out[0]
        for k in range(1, top_count):
            mixed = mixed + combine[:, k : k + 1] * picked_out[k]
        mixed = mixed.astype(jnp.bfloat16)
        grad_combine = jnp.stack(
            [jnp.sum(grad_f32 * picked_out[k], axis=1) for k in range(top_count)], axis=1
        )
        back_grads, gate_share, up_share, mixed, grad_combine = lax.optimization_barrier(
            (back_grads, gate_share, up_share, mixed, grad_combine)
        )
        picked_grads = jnp.dot(
            pick_onehot, back_grads.reshape(slots, model_width), preferred_element_type=jnp.float32
        ).reshape(top_count, tok_count, model_width)
        grad_tokens = picked_grads[0]
        for k in range(1, top_count):
            grad_tokens = grad_tokens + picked_grads[k]
        grad_tokens = grad_tokens.astype(jnp.bfloat16)
    return (mixed, grad_tokens, grad_combine, gate_share[None], up_share[None], down_share[None])


def solution(mesh):
    in_specs = (
        P(("dp", "expert"), None),
        P(("dp", "expert"), None),
        P(("dp", "expert"), None),
        P("expert", None, None),
        P("expert", None, None),
        P("expert", None, None),
        P(("dp", "expert"), None),
    )
    out_specs = (
        P(("dp", "expert"), None),
        P(("dp", "expert"), None),
        P(("dp", "expert"), None),
        P("expert", "dp", None),
        P("expert", "dp", None),
        P("expert", "dp", None),
    )
    return jax.shard_map(
        per_device, mesh=mesh, in_specs=in_specs, out_specs=out_specs, check_vma=False
    )
```

profile of v0, /device:TPU:0, one launch (start us, length us, event | category | flops | bytes accessed | tf_op | source)
XLA Modules:
  0.0 532.3 jit_solution(12989310316587515665)
XLA Ops:
  7.2 0.0 copy-start
  7.2 0.9 copy.30
  8.1 0.1 eq.51
  8.2 0.1 eq.47
  8.4 0.6 reduce-window.6
  8.9 0.2 slice_reduce_fusion
  9.2 0.1 fusion.18
  9.3 0.1 reduce_sum.39
  9.4 0.1 copy.32
  9.5 0.7 fusion.22
  10.2 0.1 fusion.14
  10.3 3.3 convolution_convert_fusion
  13.6 6.5 %all-to-all-start = ((bf16[8,64,4096]{2,1,0:T(8,128)(2,1)}), bf16[8,64,4096]{2,1,0:T(8,128)(2,1)}, u32[]{:S(2)}, u32[]{:S(2)}) async-start(bf16[8,64,4096]{2,1,0:T(8,128)(2,1)} %bitcast.69), calls=%async_computation | async-start | bytes 8388608 | tf_op jit(solution)/shard_map/all_to_all | solution.py:39
  20.1 0.1 select_reduce_fusion
  20.2 3.3 multiply_convert_fusion.1
  23.5 90.7 %all-to-all-done = bf16[8,64,4096]{2,1,0:T(8,128)(2,1)} async-done(((bf16[8,64,4096]{2,1,0:T(8,128)(2,1)}), bf16[8,64,4096]{2,1,0:T(8,128)(2,1)}, u32[]{:S(2)}, u32[]{:S(2)}) %all-to-all-start) | async-done | bytes 4194336 | tf_op jit(solution)/shard_map/all_to_all | solution.py:39
  114.2 4.7 all-to-all-start.1
  118.9 0.0 all-gather.3.cloned.1.call-start
  118.9 0.5 slice.35
  120.1 23.4 %conditional.2 = (f32[512,768]{1,0:T(8,128)}, f32[512,768]{1,0:T(8,128)}, f32[512,768]{1,0:T(8,128)}, bf16[512,768]{1,0:T(8,128)(2,1)}, bf16[512,4096]{1,0:T(8,128)(2,1)}) conditional(s32[]{:T(128)} %bitcast.8, (bf16[512,4096]{1,0:T(8,128)(2,1)}, bf16[768,4096]{1,0:T(8,128)(2,1)}, bf16[768,4096]{1,0:T(8,128)(2,1)}, ...), branch_computations={%region_5.6_spmd, %region_6.7_spmd} | conditional | flops 9666035712 | bytes 83361904
  120.4 0.0 slice-start.2
  120.4 8.8 %fusion.31 = f32[512,768]{1,0:T(8,128)} fusion(bf16[512,4096]{1,0:T(8,128)(2,1)} %get-tuple-element.27, bf16[768,4096]{1,0:T(8,128)(2,1)} %get-tuple-element.28), kind=kOutput, calls=%fused_computation.59 | convolution fusion | flops 3221225472 | bytes 12058624 | tf_op jit(solution)/shard_map/cond/branch_1_fun/dot_general | solution.py:49
  129.2 8.2 %multiply_multiply_fusion.1 = (bf16[512,768]{1,0:T(8,128)(2,1)}, f32[512,768]{1,0:T(8,128)}, f32[512,768]{1,0:T(8,128)}) fusion(f32[512,768]{1,0:T(8,128)} %fusion.31, bf16[512,4096]{1,0:T(8,128)(2,1)} %get-tuple-element.27, bf16[768,4096]{1,0:T(8,128)(2,1)S(1)} %copy-done.7), kind=kOutput, calls=%fused_computation.4 | convolution fusion | flops 3223584768 | bytes 15990784 | tf_op jit(solution)/shard_map/cond/branch_1_fun/dot_general | solution.py:50
  137.4 6.1 %fusion.32 = bf16[512,4096]{1,0:T(8,128)(2,1)} fusion(bf16[512,768]{1,0:T(8,128)(2,1)} %get-tuple-element.84, bf16[768,4096]{1,0:T(8,128)(2,1)S(1)} %bitcast.83), kind=kOutput, calls=%fused_computation.60 | convolution fusion | flops 3221225472 | bytes 11272192 | tf_op jit(solution)/shard_map/cond/branch_1_fun/dot_general | solution.py:53
  143.5 69.4 %all-to-all-done.1 = bf16[8,64,4096]{2,1,0:T(8,128)(2,1)} async-done(((bf16[8,64,4096]{2,1,0:T(8,128)(2,1)}), bf16[8,64,4096]{2,1,0:T(8,128)(2,1)}, u32[]{:S(2)}, u32[]{:S(2)}) %all-to-all-start.1) | async-done | bytes 4194336 | tf_op jit(solution)/shard_map/all_to_all | solution.py:41
  212.9 9.1 %multiply_convert_fusion.2 = (bf16[512,768]{1,0:T(8,128)(2,1)S(1)}, bf16[512,768]{1,0:T(8,128)(2,1)S(1)}) fusion(f32[512,768]{1,0:T(8,128)} %get-tuple-element.52, f32[512,768]{1,0:T(8,128)} %get-tuple-element.53, f32[512,768]{1,0:T(8,128)} %get-tuple-element.51, bf16[512,4096]{1,0:T(8,128)(2,1)} %bitcast.6, bf16[1,768,4096]{2,1,0:T(8,128)(2,1)} %param.14), kind=kOutput, calls=%fused_computation.24 | convolution fusion | flops 3225157632 | bytes 16777216 | tf_op jit(solution)/shard_map/dot_general | solution.py:70
  221.9 1.3 pad_maximum_fusion
  223.2 0.0 all-gather.3.cloned.1.call-update
  223.2 0.0 all-gather.5.cloned.1.call-start
  223.3 0.7 all-gather.5.cloned.1.call-update
  224.0 4.6 all-to-all-start.3
  228.6 0.5 reduce-scatter.2.cloned.1.call-start
  229.1 9.2 %multiply_convert_fusion = bf16[768,4096]{1,0:T(8,128)(2,1)} fusion(bf16[512,4096]{1,0:T(8,128)(2,1)} %bitcast.6, bf16[512,768]{1,0:T(8,128)(2,1)} %get-tuple-element.60), kind=kOutput, calls=%fused_computation.8 | convolution fusion | flops 3227516928 | bytes 11272192 | tf_op jit(solution)/shard_map/weight_grads/rf,rd->fd/dot_general | solution.py:90
  238.3 0.0 reduce-scatter.2.cloned.1.call-update
  238.3 5.5 %fusion.25 = f32[512,4096]{1,0:T(8,128)S(1)} fusion(bf16[512,768]{1,0:T(8,128)(2,1)S(1)} %get-tuple-element.70, bf16[1,768,4096]{2,1,0:T(8,128)(2,1)} %param.12), kind=kOutput, calls=%fused_computation.53 | convolution fusion | flops 3221225472 | bytes 15466496 | tf_op jit(solution)/shard_map/dot_general | solution.py:76
  243.8 7.8 %add_convert_fusion = bf16[512,4096]{1,0:T(8,128)(2,1)} fusion(f32[512,4096]{1,0:T(8,128)S(1)} %fusion.25, bf16[512,768]{1,0:T(8,128)(2,1)S(1)} %get-tuple-element.69, bf16[1,768,4096]{2,1,0:T(8,128)(2,1)} %param.13), kind=kOutput, calls=%fused_computation.9 | convolution fusion | flops 3225419776 | bytes 19660800 | tf_op jit(solution)/shard_map/dot_general | solution.py:77
  251.7 70.9 %all-to-all-done.3 = bf16[8,64,4096]{2,1,0:T(8,128)(2,1)} async-done(((bf16[8,64,4096]{2,1,0:T(8,128)(2,1)}), bf16[8,64,4096]{2,1,0:T(8,128)(2,1)}, u32[]{:S(2)}, u32[]{:S(2)}) %all-to-all-start.3) | async-done | bytes 4194336 | tf_op jit(solution)/shard_map/all_to_all | solution.py:62
  322.6 4.7 all-to-all-start.2
  327.3 3.5 fusion.13
  330.8 2.0 fusion.6
  332.8 0.6 pad_maximum_fusion.1
  333.4 118.3 %all-gather.5.cloned.1.call-done = bf16[2048,4096]{1,0:T(8,128)(2,1)} async-done(((bf16[512,4096]{1,0:T(8,128)(2,1)}), bf16[2048,4096]{1,0:T(8,128)(2,1)}) %all-gather.5.cloned.1.call-update) | async-done | bytes 16777232 | tf_op jit(solution)/shard_map/weight_grads/all_gather | solution.py:92
  451.7 11.2 %fusion.5 = bf16[192,4096]{1,0:T(8,128)(2,1)} fusion(bf16[2048,4096]{1,0:T(8,128)(2,1)} %all-gather.5.cloned.1.call-done, bf16[2048,1536]{1,0:T(8,128)(2,1)} %all-gather.3.cloned.1.call-done, s32[]{:T(128)S(6)} %select_n.12), kind=kOutput, calls=%fused_computation.15 | convolution fusion | flops 3222798336 | bytes 19398660 | tf_op jit(solution)/shard_map/weight_grads/rf,rd->fd/dot_general | solution.py:103
  462.9 1.0 copy-done.2
  464.0 6.2 %fusion.4 = bf16[192,4096]{1,0:T(8,128)(2,1)} fusion(bf16[2048,4096]{1,0:T(8,128)(2,1)S(1)} %copy-done.2, bf16[2048,1536]{1,0:T(8,128)(2,1)} %all-gather.3.cloned.1.call-done, s32[]{:T(128)S(6)} %select_n.11), kind=kOutput, calls=%fused_computation.14 | convolution fusion | flops 3222798336 | bytes 19398660 | tf_op jit(solution)/shard_map/weight_grads/rf,rd->fd/dot_general | solution.py:100
  470.2 3.6 fusion.12
  473.8 1.2 fusion.8
  475.0 50.6 %reduce-scatter.2.cloned.1.call-done = bf16[192,4096]{1,0:T(8,128)(2,1)} async-done(((bf16[768,4096]{1,0:T(8,128)(2,1)}), bf16[192,4096]{1,0:T(8,128)(2,1)}) %reduce-scatter.2.cloned.1.call-update) | async-done | bytes 1572880 | tf_op jit(solution)/shard_map/reduce_scatter | solution.py:105
  (22 shorter events, 0.1 us)
Async XLA Ops:
  7.2 3.2 copy-start
  13.6 6.5 %copy-start.5 = (f32[128,2]{0,1:T(2,128)S(1)}, f32[128,2]{0,1:T(2,128)}, u32[]{:S(2)}) copy-start(f32[128,2]{0,1:T(2,128)} %param.11) | copy-start | bytes 3076
  13.6 6.6 %copy-start.3 = (bf16[128,4096]{1,0:T(8,128)(2,1)S(1)}, bf16[128,4096]{1,0:T(8,128)(2,1)}, u32[]{:S(2)}) copy-start(bf16[128,4096]{1,0:T(8,128)(2,1)} %param.15) | copy-start | bytes 3145732
  13.6 100.6 %all-to-all-start = ((bf16[8,64,4096]{2,1,0:T(8,128)(2,1)}), bf16[8,64,4096]{2,1,0:T(8,128)(2,1)}, u32[]{:S(2)}, u32[]{:S(2)}) async-start(bf16[8,64,4096]{2,1,0:T(8,128)(2,1)} %bitcast.69), calls=%async_computation | async-start | bytes 8388608 | tf_op jit(solution)/shard_map/all_to_all | solution.py:39
  114.2 4.7 copy-start.4
  114.2 98.7 %all-to-all-start.1 = ((bf16[8,64,4096]{2,1,0:T(8,128)(2,1)}), bf16[8,64,4096]{2,1,0:T(8,128)(2,1)}, u32[]{:S(2)}, u32[]{:S(2)}) async-start(bf16[8,64,4096]{2,1,0:T(8,128)(2,1)} %bitcast.68), calls=%async_computation.1 | async-start | bytes 8388608 | tf_op jit(solution)/shard_map/all_to_all | solution.py:41
  118.9 214.5 %all-gather.3.cloned.1.call-start = ((), (), s32[]{:S(2)}) async-start(), calls=%async_computation.5 | async-start | bytes 7864320 | tf_op jit(solution)/shard_map/weight_grads/all_gather | solution.py:94
  120.4 8.8 %copy-start.7 = (bf16[768,4096]{1,0:T(8,128)(2,1)S(1)}, bf16[768,4096]{1,0:T(8,128)(2,1)}, u32[]{:S(2)}) copy-start(bf16[768,4096]{1,0:T(8,128)(2,1)} %get-tuple-element.29) | copy-start | bytes 18874372 | tf_op jit(solution)/shard_map/conditional
  120.4 17.0 %slice-start.2 = ((s8[6291456]{0:T(1024)(128)(4,1)}), s8[4194304]{0:T(1024)(128)(4,1)S(1)}, s32[]{:S(2)}) async-start(s8[6291456]{0:T(1024)(128)(4,1)} %bitcast.82), calls=%async_computation.10 | async-start | bytes 8388608 | tf_op jit(solution)/shard_map/conditional
  129.2 8.2 %slice-start.3 = ((s8[6291456]{0:T(1024)(128)(4,1)}), s8[2097152]{0:T(1024)(128)(4,1)S(1)}, s32[]{:S(2)}) async-start(s8[6291456]{0:T(1024)(128)(4,1)} %bitcast.82), calls=%async_computation.11 | async-start | bytes 4194304 | tf_op jit(solution)/shard_map/conditional
  223.2 228.5 %all-gather.5.cloned.1.call-start = ((), (), s32[]{:S(2)}) async-start(), calls=%async_computation.6 | async-start | bytes 20971520 | tf_op jit(solution)/shard_map/weight_grads/all_gather | solution.py:92
  224.0 98.6 %all-to-all-start.3 = ((bf16[8,64,4096]{2,1,0:T(8,128)(2,1)}), bf16[8,64,4096]{2,1,0:T(8,128)(2,1)}, u32[]{:S(2)}, u32[]{:S(2)}) async-start(bf16[8,64,4096]{2,1,0:T(8,128)(2,1)} %bitcast.15), calls=%async_computation.3 | async-start | bytes 8388608 | tf_op jit(solution)/shard_map/all_to_all | solution.py:62
  228.6 297.0 %reduce-scatter.2.cloned.1.call-start = ((), (), s32[]{:S(2)}) async-start(), calls=%async_computation.7 | async-start | bytes 7864320 | tf_op jit(solution)/shard_map/reduce_scatter | solution.py:105
  322.6 147.6 %all-to-all-start.2 = ((bf16[8,64,4096]{2,1,0:T(8,128)(2,1)}), bf16[8,64,4096]{2,1,0:T(8,128)(2,1)}, u32[]{:S(2)}, u32[]{:S(2)}) async-start(bf16[8,64,4096]{2,1,0:T(8,128)(2,1)} %bitcast.72), calls=%async_computation.2 | async-start | bytes 8388608 | tf_op jit(solution)/shard_map/all_to_all | solution.py:79
  451.7 12.2 %copy-start.2 = (bf16[2048,4096]{1,0:T(8,128)(2,1)S(1)}, bf16[2048,4096]{1,0:T(8,128)(2,1)}, u32[]{:S(2)}) copy-start(bf16[2048,4096]{1,0:T(8,128)(2,1)} %all-gather.5.cloned.1.call-done) | copy-start | bytes 50331652
  470.2 55.4 %copy-start.1 = (bf16[128,4096]{1,0:T(8,128)(2,1)S(1)}, bf16[128,4096]{1,0:T(8,128)(2,1)}, u32[]{:S(2)}) copy-start(bf16[128,4096]{1,0:T(8,128)(2,1)} %param.9) | copy-start | bytes 3145732
Sparse Core Ops, SparseCore 0:
  223.3 69.0 all-gather.2
  294.3 157.4 all-gather.4
  455.3 70.2 reduce-scatter.1
where the time goes:
time: 540 us; the launch traced here: 532 us
  waiting for transfers between devices  401 us (74%)
  matrix products  85.7 us (16%)
  starting transfers between devices  21 us (4%)
  between operations  14.7 us (3%)
  other arithmetic  6.73 us (1%)
    all_gather x1, waiting for transfers between devices, per_device(): rows_all = lax.all_gather(in_rows, 'dp', axis=0, tiled=True)  118 us
    all_to_all x1, waiting for transfers between devices, per_device(): lax.all_to_all(send_rows, 'expert', split_axis=0, concat_axis=0, tiled=True)  90.7 us
    all_to_all x1, waiting for transfers between devices, per_device(): lax.all_to_all(expert_out.reshape(experts, capacity, model_width), 'exper...  70.9 us
    all_to_all x1, waiting for transfers between devices, per_device(): lax.all_to_all(send_grads, 'expert', split_axis=0, concat_axis=0, tiled=T...  69.4 us
    reduce_scatter x1, waiting for transfers between devices, per_device(): lax.psum_scatter(down_term, 'dp', scatter_dimension=0, tiled=True)  50.6 us
    dot_general x1, matrix products, per_device(): jnp.einsum('rf,rd->fd', up_cols, rows_all, preferred_element_type=jnp.flo...  11.2 us
  transfers between devices with their start and end apart: 7, of which 5 were waited for; matrix products, arithmetic and copies ran while one was open for 15% of the time, Pallas kernels for 0%

commit v1 on v0

--- a/solution.py
+++ b/solution.py
@@ -2,6 +2,25 @@
 import jax.numpy as jnp
 from jax import lax
 from jax.sharding import PartitionSpec as P
+
+
+def ring_gather(x, axis, dim):
+    size, index, rows = (lax.axis_size(axis), lax.axis_index(axis), x.shape[dim])
+    ahead = [(i, (i + 1) % size) for i in range(size)]
+    downward = [(i, (i - 1) % size) for i in range(size)]
+    out = jnp.zeros((*x.shape[:dim], size * rows, *x.shape[dim + 1 :]), x.dtype)
+    out = lax.dynamic_update_slice_in_dim(out, x, index * rows, axis=dim)
+    from_left = from_right = x
+    halfway = size // 2
+    for lap in range(1, halfway + 1):
+        from_left = lax.ppermute(from_left, axis, ahead)
+        out = lax.dynamic_update_slice_in_dim(out, from_left, (index - lap) % size * rows, axis=dim)
+        if lap < size - halfway:
+            from_right = lax.ppermute(from_right, axis, downward)
+            out = lax.dynamic_update_slice_in_dim(
+                out, from_right, (index + lap) % size * rows, axis=dim
+            )
+    return out
 
 
 def slot_targets(expert_ids, experts, capacity):
@@ -89,7 +108,7 @@
             scale
             * jnp.einsum("rf,rd->fd", activated, out_grads, preferred_element_type=jnp.float32)
         ).astype(jnp.bfloat16)
-        rows_all = lax.all_gather(in_rows, "dp", axis=0, tiled=True)
+        rows_all = ring_gather(in_rows, "dp", 0)
         grads_pre = jnp.concatenate([grad_gate_pre, grad_up_pre], axis=1)
         grads_all = lax.all_gather(grads_pre, "dp", axis=0, tiled=True)
         me_dp = lax.axis_index("dp")

time: 540 us -> 652 us (1.21)
  waiting for transfers between devices: 401 us -> 469 us
  local copies, waits for them, and re-layouts: 3.18 us -> 26.8 us
  loops' own time: 0.29 us -> 11.8 us
    ppermute x0 -> x3, waiting for transfers between devices: none -> 253 us  [the longest x2 155 us: ring_gather(): from_left = lax.ppermute(from_left, axis, ahead)]
    all_gather x1 -> x0, waiting for transfers between devices: 118 us -> none  [per_device(): rows_all = lax.all_gather(in_rows, 'dp', axis=0, tiled=True)]
    reduce_scatter x1, waiting for transfers between devices: 50.6 us -> 0.01 us  [per_device(): lax.psum_scatter(down_term, 'dp', scatter_dimension=0, tiled=True)]
    dynamic_update_slice x0 -> x4, local copies, waits for them, and re-layouts: none -> 18.7 us  [the longest x2 9.26 us: ring_gather(): lax.dynamic_update_slice_in_dim(out, from_left, (index - lap) % size * ro...]
    all_to_all x1, waiting for transfers between devices: 69.4 us -> 57.7 us  [per_device(): lax.all_to_all(send_grads, 'expert', split_axis=0, concat_axis=0, tiled=T...]
    unnamed x1, loops' own time: 0.29 us -> 11.8 us
  transfers between devices with their start and end apart: 7 -> 9, of which waited for: 5 -> 6; matrix products, arithmetic and copies ran while one was open for 15% -> 17% of each run, Pallas kernels for 0% -> 0%
where the time goes in v1:
time: 652 us; the launch traced here: 644 us
  waiting for transfers between devices  469 us (72%)
  matrix products  90.5 us (14%)
  local copies, waits for them, and re-layouts  26.8 us (4%)
  starting transfers between devices  23.3 us (4%)
  between operations  15.2 us (2%)
  loops' own time  11.8 us (2%)
  other arithmetic  6.73 us (1%)
    ppermute x2, waiting for transfers between devices, ring_gather(): from_left = lax.ppermute(from_left, axis, ahead)  155 us
    ppermute x1, waiting for transfers between devices, ring_gather(): from_right = lax.ppermute(from_right, axis, downward)  97.8 us
    all_to_all x1, waiting for transfers between devices, per_device(): lax.all_to_all(send_rows, 'expert', split_axis=0, concat_axis=0, tiled=True)  90.7 us
    all_to_all x1, waiting for transfers between devices, per_device(): lax.all_to_all(expert_out.reshape(experts, capacity, model_width), 'exper...  68.3 us
    all_to_all x1, waiting for transfers between devices, per_device(): lax.all_to_all(send_grads, 'expert', split_axis=0, concat_axis=0, tiled=T...  57.7 us
  transfers between devices with their start and end apart: 9, of which 6 were waited for; matrix products, arithmetic and copies ran while one was open for 17% of the time, Pallas kernels for 0%

profile of v1, /device:TPU:0, one launch (start us, length us, event | category | flops | bytes accessed | tf_op | source)
XLA Modules:
  0.0 643.8 jit_solution(10339565204439641524)
XLA Ops:
  7.2 0.9 copy.30
  8.1 0.1 eq.55
  8.2 0.1 eq.51
  8.4 0.6 reduce-window.6
  8.9 0.2 slice_reduce_fusion
  9.2 0.1 fusion.18
  9.3 0.1 reduce_sum.39
  9.4 0.1 copy.32
  9.5 0.7 fusion.22
  10.2 0.1 fusion.14
  10.3 3.3 convolution_convert_fusion
  13.6 6.5 %all-to-all-start = ((bf16[8,64,4096]{2,1,0:T(8,128)(2,1)}), bf16[8,64,4096]{2,1,0:T(8,128)(2,1)}, u32[]{:S(2)}, u32[]{:S(2)}) async-start(bf16[8,64,4096]{2,1,0:T(8,128)(2,1)} %bitcast.69), calls=%async_computation | async-start | bytes 8388608 | tf_op jit(solution)/shard_map/all_to_all | solution.py:58
  20.1 0.1 select_reduce_fusion
  20.2 3.2 multiply_convert_fusion.1
  23.5 90.7 %all-to-all-done = bf16[8,64,4096]{2,1,0:T(8,128)(2,1)} async-done(((bf16[8,64,4096]{2,1,0:T(8,128)(2,1)}), bf16[8,64,4096]{2,1,0:T(8,128)(2,1)}, u32[]{:S(2)}, u32[]{:S(2)}) %all-to-all-start) | async-done | bytes 4194336 | tf_op jit(solution)/shard_map/all_to_all | solution.py:58
  114.2 4.7 all-to-all-start.1
  118.9 0.5 slice.35
  120.1 35.1 %conditional.2 = (f32[512,768]{1,0:T(8,128)}, f32[512,768]{1,0:T(8,128)}, f32[512,768]{1,0:T(8,128)}, bf16[512,768]{1,0:T(8,128)(2,1)}, bf16[512,4096]{1,0:T(8,128)(2,1)}) conditional(s32[]{:T(128)} %bitcast.8, (bf16[512,4096]{1,0:T(8,128)(2,1)}, bf16[768,4096]{1,0:T(8,128)(2,1)}, bf16[768,4096]{1,0:T(8,128)(2,1)}, ...), branch_computations={%region_5.6_spmd, %region_6.7_spmd} | conditional | flops 9666035712 | bytes 83361904
  131.9 8.8 %fusion.31 = f32[512,768]{1,0:T(8,128)} fusion(bf16[512,4096]{1,0:T(8,128)(2,1)} %get-tuple-element.27, bf16[768,4096]{1,0:T(8,128)(2,1)} %get-tuple-element.28), kind=kOutput, calls=%fused_computation.63 | convolution fusion | flops 3221225472 | bytes 12058624 | tf_op jit(solution)/shard_map/cond/branch_1_fun/dot_general | solution.py:68
  140.7 8.2 %multiply_multiply_fusion.1 = (bf16[512,768]{1,0:T(8,128)(2,1)}, f32[512,768]{1,0:T(8,128)}, f32[512,768]{1,0:T(8,128)}) fusion(f32[512,768]{1,0:T(8,128)} %fusion.31, bf16[512,4096]{1,0:T(8,128)(2,1)} %get-tuple-element.27, bf16[768,4096]{1,0:T(8,128)(2,1)S(1)} %copy-done.6), kind=kOutput, calls=%fused_computation.4 | convolution fusion | flops 3223584768 | bytes 15990784 | tf_op jit(solution)/shard_map/cond/branch_1_fun/dot_general | solution.py:69
  148.9 6.2 fusion.32
  155.2 57.7 %all-to-all-done.1 = bf16[8,64,4096]{2,1,0:T(8,128)(2,1)} async-done(((bf16[8,64,4096]{2,1,0:T(8,128)(2,1)}), bf16[8,64,4096]{2,1,0:T(8,128)(2,1)}, u32[]{:S(2)}, u32[]{:S(2)}) %all-to-all-start.1) | async-done | bytes 4194336 | tf_op jit(solution)/shard_map/all_to_all | solution.py:60
  212.9 8.9 %multiply_convert_fusion.2 = (bf16[512,768]{1,0:T(8,128)(2,1)S(1)}, bf16[512,768]{1,0:T(8,128)(2,1)S(1)}) fusion(f32[512,768]{1,0:T(8,128)} %get-tuple-element.52, f32[512,768]{1,0:T(8,128)} %get-tuple-element.53, f32[512,768]{1,0:T(8,128)} %get-tuple-element.51, bf16[512,4096]{1,0:T(8,128)(2,1)} %bitcast.6, bf16[1,768,4096]{2,1,0:T(8,128)(2,1)} %param.14), kind=kOutput, calls=%fused_computation.24 | convolution fusion | flops 3225157632 | bytes 16777216 | tf_op jit(solution)/shard_map/dot_general | solution.py:89
  221.8 1.3 pad_maximum_fusion
  223.1 4.6 all-to-all-start.3
  227.7 0.0 reduce-scatter.2.cloned.1.call-start
  227.7 9.3 %multiply_convert_fusion = bf16[768,4096]{1,0:T(8,128)(2,1)} fusion(bf16[512,4096]{1,0:T(8,128)(2,1)} %bitcast.6, bf16[512,768]{1,0:T(8,128)(2,1)} %get-tuple-element.60), kind=kOutput, calls=%fused_computation.8 | convolution fusion | flops 3227516928 | bytes 11272192 | tf_op jit(solution)/shard_map/weight_grads/rf,rd->fd/dot_general | solution.py:109
  237.1 1.4 collective-permute-start
  238.5 1.5 collective-permute-start.1
  240.0 5.5 fusion.25
  245.6 7.8 %add_convert_fusion = bf16[512,4096]{1,0:T(8,128)(2,1)} fusion(f32[512,4096]{1,0:T(8,128)S(1)} %fusion.25, bf16[512,768]{1,0:T(8,128)(2,1)S(1)} %get-tuple-element.69, bf16[1,768,4096]{2,1,0:T(8,128)(2,1)} %param.13), kind=kOutput, calls=%fused_computation.9 | convolution fusion | flops 3225419776 | bytes 19660800 | tf_op jit(solution)/shard_map/dot_general | solution.py:96
  253.4 68.3 %all-to-all-done.3 = bf16[8,64,4096]{2,1,0:T(8,128)(2,1)} async-done(((bf16[8,64,4096]{2,1,0:T(8,128)(2,1)}), bf16[8,64,4096]{2,1,0:T(8,128)(2,1)}, u32[]{:S(2)}, u32[]{:S(2)}) %all-to-all-start.3) | async-done | bytes 4194336 | tf_op jit(solution)/shard_map/all_to_all | solution.py:81
  321.7 4.5 all-to-all-start.2
  326.2 75.0 %collective-permute-done = bf16[512,4096]{1,0:T(8,128)(2,1)} collective-permute-done((bf16[512,4096]{1,0:T(8,128)(2,1)}, bf16[512,4096]{1,0:T(8,128)(2,1)}, u32[]{:S(2)}, u32[]{:S(2)}) %collective-permute-start) | collective-permute-done | bytes 4194336 | tf_op jit(solution)/shard_map/weight_grads/ppermute | solution.py:16
  401.2 6.0 broadcast_in_dim.31
  407.2 4.8 constant_dynamic-update-slice_fusion.3
  412.0 4.6 constant_dynamic-update-slice_fusion.2
  416.6 97.8 %collective-permute-done.1 = bf16[512,4096]{1,0:T(8,128)(2,1)} collective-permute-done((bf16[512,4096]{1,0:T(8,128)(2,1)}, bf16[512,4096]{1,0:T(8,128)(2,1)}, u32[]{:S(2)}, u32[]{:S(2)}) %collective-permute-start.1) | collective-permute-done | bytes 4194336 | tf_op jit(solution)/shard_map/weight_grads/ppermute | solution.py:19
  514.4 4.7 constant_dynamic-update-slice_fusion.1
  519.1 3.5 fusion.13
  522.6 2.0 fusion.6
  524.6 0.6 pad_maximum_fusion.1
  525.2 79.9 %collective-permute-done.2 = bf16[512,4096]{1,0:T(8,128)(2,1)} collective-permute-done((bf16[512,4096]{1,0:T(8,128)(2,1)}, bf16[512,4096]{1,0:T(8,128)(2,1)}, u32[]{:S(2)}, u32[]{:S(2)}) %collective-permute-start.2) | collective-permute-done | bytes 4194336 | tf_op jit(solution)/shard_map/weight_grads/ppermute | solution.py:16
  605.0 4.7 constant_dynamic-update-slice_fusion
  609.7 11.1 %fusion.5 = bf16[192,4096]{1,0:T(8,128)(2,1)} fusion(bf16[2048,4096]{1,0:T(8,128)(2,1)} %constant_dynamic-update-slice_fusion, bf16[2048,1536]{1,0:T(8,128)(2,1)} %all-gather.2.cloned.1.call-done, s32[]{:T(128)S(6)} %select_n.46), kind=kOutput, calls=%fused_computation.15 | convolution fusion | flops 3222798336 | bytes 19398660 | tf_op jit(solution)/shard_map/weight_grads/rf,rd->fd/dot_general | solution.py:122
  620.7 11.1 %fusion.4 = bf16[192,4096]{1,0:T(8,128)(2,1)} fusion(bf16[2048,4096]{1,0:T(8,128)(2,1)} %constant_dynamic-update-slice_fusion, bf16[2048,1536]{1,0:T(8,128)(2,1)} %all-gather.2.cloned.1.call-done, s32[]{:T(128)S(6)} %select_n.38), kind=kOutput, calls=%fused_computation.14 | convolution fusion | flops 3222798336 | bytes 19398660 | tf_op jit(solution)/shard_map/weight_grads/rf,rd->fd/dot_general | solution.py:119
  631.8 3.6 fusion.12
  635.4 1.2 fusion.8
  (28 shorter events, 0.2 us)
Async XLA Ops:
  7.2 3.2 copy-start
  13.6 6.5 %copy-start.4 = (f32[128,2]{0,1:T(2,128)S(1)}, f32[128,2]{0,1:T(2,128)}, u32[]{:S(2)}) copy-start(f32[128,2]{0,1:T(2,128)} %param.11) | copy-start | bytes 3076
  13.6 6.6 %copy-start.2 = (bf16[128,4096]{1,0:T(8,128)(2,1)S(1)}, bf16[128,4096]{1,0:T(8,128)(2,1)}, u32[]{:S(2)}) copy-start(bf16[128,4096]{1,0:T(8,128)(2,1)} %param.15) | copy-start | bytes 3145732
  13.6 100.6 %all-to-all-start = ((bf16[8,64,4096]{2,1,0:T(8,128)(2,1)}), bf16[8,64,4096]{2,1,0:T(8,128)(2,1)}, u32[]{:S(2)}, u32[]{:S(2)}) async-start(bf16[8,64,4096]{2,1,0:T(8,128)(2,1)} %bitcast.69), calls=%async_computation | async-start | bytes 8388608 | tf_op jit(solution)/shard_map/all_to_all | solution.py:58
  114.2 4.7 copy-start.3
  114.2 98.7 %all-to-all-start.1 = ((bf16[8,64,4096]{2,1,0:T(8,128)(2,1)}), bf16[8,64,4096]{2,1,0:T(8,128)(2,1)}, u32[]{:S(2)}, u32[]{:S(2)}) async-start(bf16[8,64,4096]{2,1,0:T(8,128)(2,1)} %bitcast.68), calls=%async_computation.1 | async-start | bytes 8388608 | tf_op jit(solution)/shard_map/all_to_all | solution.py:60
  118.9 490.8 %all-gather.2.cloned.1.call-start = ((), (), s32[]{:S(2)}) async-start(), calls=%async_computation.5 | async-start | bytes 7864320 | tf_op jit(solution)/shard_map/weight_grads/all_gather | solution.py:113
  131.9 8.8 %copy-start.6 = (bf16[768,4096]{1,0:T(8,128)(2,1)S(1)}, bf16[768,4096]{1,0:T(8,128)(2,1)}, u32[]{:S(2)}) copy-start(bf16[768,4096]{1,0:T(8,128)(2,1)} %get-tuple-element.29) | copy-start | bytes 18874372 | tf_op jit(solution)/shard_map/conditional
  131.9 17.0 %slice-start.2 = ((s8[6291456]{0:T(1024)(128)(4,1)}), s8[4194304]{0:T(1024)(128)(4,1)S(1)}, s32[]{:S(2)}) async-start(s8[6291456]{0:T(1024)(128)(4,1)} %bitcast.82), calls=%async_computation.9 | async-start | bytes 8388608 | tf_op jit(solution)/shard_map/conditional
  140.7 8.2 %slice-start.3 = ((s8[6291456]{0:T(1024)(128)(4,1)}), s8[2097152]{0:T(1024)(128)(4,1)S(1)}, s32[]{:S(2)}) async-start(s8[6291456]{0:T(1024)(128)(4,1)} %bitcast.82), calls=%async_computation.10 | async-start | bytes 4194304 | tf_op jit(solution)/shard_map/conditional
  223.1 98.6 %all-to-all-start.3 = ((bf16[8,64,4096]{2,1,0:T(8,128)(2,1)}), bf16[8,64,4096]{2,1,0:T(8,128)(2,1)}, u32[]{:S(2)}, u32[]{:S(2)}) async-start(bf16[8,64,4096]{2,1,0:T(8,128)(2,1)} %bitcast.15), calls=%async_computation.3 | async-start | bytes 8388608 | tf_op jit(solution)/shard_map/all_to_all | solution.py:81
  227.7 408.9 %reduce-scatter.2.cloned.1.call-start = ((), (), s32[]{:S(2)}) async-start(), calls=%async_computation.6 | async-start | bytes 7864320 | tf_op jit(solution)/shard_map/reduce_scatter | solution.py:124
  237.1 164.1 %collective-permute-start = (bf16[512,4096]{1,0:T(8,128)(2,1)}, bf16[512,4096]{1,0:T(8,128)(2,1)}, u32[]{:S(2)}, u32[]{:S(2)}) collective-permute-start(bf16[512,4096]{1,0:T(8,128)(2,1)} %bitcast.9), channel_id=1, source_target_pairs={{0,8},{8,16},{16,24},{24,0},{1,9},{9,17},{17,25},{25,1},{2,10},{10... | collective-permute-start | bytes 12582920 | tf_op jit(solution)/shard_map/weight_grads/ppermute | solution.py:16
  238.5 275.9 %collective-permute-start.1 = (bf16[512,4096]{1,0:T(8,128)(2,1)}, bf16[512,4096]{1,0:T(8,128)(2,1)}, u32[]{:S(2)}, u32[]{:S(2)}) collective-permute-start(bf16[512,4096]{1,0:T(8,128)(2,1)} %bitcast.9), channel_id=1, source_target_pairs={{0,24},{8,0},{16,8},{24,16},{1,25},{9,1},{17,9},{25,17},{2,26},{10... | collective-permute-start | bytes 12582920 | tf_op jit(solution)/shard_map/weight_grads/ppermute | solution.py:19
  321.7 310.1 %all-to-all-start.2 = ((bf16[8,64,4096]{2,1,0:T(8,128)(2,1)}), bf16[8,64,4096]{2,1,0:T(8,128)(2,1)}, u32[]{:S(2)}, u32[]{:S(2)}) async-start(bf16[8,64,4096]{2,1,0:T(8,128)(2,1)} %bitcast.72), calls=%async_computation.2 | async-start | bytes 8388608 | tf_op jit(solution)/shard_map/all_to_all | solution.py:98
  401.2 203.8 %collective-permute-start.2 = (bf16[512,4096]{1,0:T(8,128)(2,1)}, bf16[512,4096]{1,0:T(8,128)(2,1)}, u32[]{:S(2)}, u32[]{:S(2)}) collective-permute-start(bf16[512,4096]{1,0:T(8,128)(2,1)} %collective-permute-done), channel_id=1, source_target_pairs={{0,8},{8,16},{16,24},{24,0},{1,9},{9,17},{17,25},{25,1},{2,10},{10... | collective-permute-start | bytes 12582920 | tf_op jit(solution)/shard_map/weight_grads/ppermute | solution.py:16
  631.8 4.8 copy-start.1
Sparse Core Ops, SparseCore 0:
  223.2 112.9 all-gather.1
  339.8 119.7 reduce-scatter.1
